TPU v7x, 128 devices: a whole 4x4x4 slice. The times are simulated.
128 devices in a mesh: req: 32 (over z, x, y_hi), tp: 4 (over y_lo, core).
Axes of the slice: x: 4, y: 4 (y_hi: 2, y_lo: 2; y = y_hi * 2 + y_lo), z: 4, core: 2. Of those that a mesh axis runs over, the one named last changes fastest.
Arguments:
- hidden_in: bfloat16 [64, 512, 1280], P('req'), may hold values from -6 to 6
- lengths: int32 [64], P('req'), may hold values from 128 to 512, as said below
- attn_gain: float32 [1280], replicated, may hold values from 0.1 to 1.9
- mlp_gain: float32 [1280], replicated, may hold values from 0.1 to 1.9
- q_master: float32 [1280, 1280], P(('req', 'tp')), may hold values from -1 to 1
- k_master: float32 [1280, 320], P(('req', 'tp')), may hold values from -1 to 1
- trainer_value_weight: float32 [1280, 320], P(('req', 'tp')), may hold values from -0.15625 to 0.15625
- o_master: float32 [1280, 1280], P(('req', 'tp')), may hold values from -0.15625 to 0.15625
- gate_master: float32 [1280, 3584], P(('req', 'tp')), may hold values from -0.15625 to 0.15625
- up_master: float32 [1280, 3584], P(('req', 'tp')), may hold values from -0.15625 to 0.15625
- down_master: float32 [3584, 1280], P(('req', 'tp')), may hold values from -0.09375 to 0.09375
Outputs:
- hidden_out: bfloat16 [64, 512, 1280], P('req')
- kv_cache: bfloat16 [64, 512, 640], P('req')
Inputs may be any that keep to these rules, and one draw needn't show every extreme that they name: `lengths`: each prompt has at least a quarter of 512 real tokens; in every draw some prompt has exactly 512.
All inputs are finite; a program needn't handle non-finite values.
Results may differ from a plain program's by a relative error of at most 0.012.
Values may be sent and summed in bfloat16 or wider, within the bound.
No kernel may reach another device: no remote copies, remote signals or barrier semaphores. Data moves between devices by JAX's collectives and lax.ppermute only.
A program may use at most 192 MiB of HBM per device.

v0:
```python
import math

import jax
import jax.numpy as jnp
from jax import lax
from jax.sharding import PartitionSpec as P

QUERY_HEADS = 20
KEY_VALUE_HEADS = 5
HEAD_DIM = 64


def rms_norm(field, gain_vec):
    scale = lax.rsqrt(jnp.mean(field * field, axis=-1, keepdims=True) + 1e-05)
    return (field * scale * gain_vec).astype(jnp.bfloat16)


def rope_tables(sequence_length, head_size):
    half_width = head_size // 2
    positions = jnp.arange(sequence_length, dtype=jnp.float32)[:, None]
    frequency = jnp.exp(
        -math.log(10000.0) * (2.0 * jnp.arange(half_width, dtype=jnp.float32) / head_size)
    )
    angles = positions * frequency[None, :]
    return (jnp.cos(angles), jnp.sin(angles))


def rotate(field, cosine_table, sine_table):
    half_width = field.shape[-1] // 2
    first_half = field[..., :half_width]
    second_half = field[..., half_width:]
    cos_b = cosine_table[:, None, :]
    sin_b = sine_table[:, None, :]
    return jnp.concatenate(
        [first_half * cos_b - second_half * sin_b, second_half * cos_b + first_half * sin_b],
        axis=-1,
    )


def local(
    hidden_in,
    lengths,
    attn_gain,
    mlp_gain,
    q_master,
    k_master,
    trainer_value_weight,
    o_master,
    gate_master,
    up_master,
    down_master,
):
    tp_count = lax.axis_size("tp")
    tensor_shard_index = lax.axis_index("tp")
    q_cast = q_master.astype(jnp.bfloat16)
    k_cast = k_master.astype(jnp.bfloat16)
    v_cast = trainer_value_weight.astype(jnp.bfloat16)
    o_cast = o_master.astype(jnp.bfloat16)
    gate_cast = gate_master.astype(jnp.bfloat16)
    up_cast = up_master.astype(jnp.bfloat16)
    down_cast = down_master.astype(jnp.bfloat16)
    q_cols = q_master.shape[1] // tp_count
    ff_cols = gate_master.shape[1] // tp_count
    q_full, key_weight, value_weight, o_full, gate_full, up_full, down_full = (
        lax.all_gather(q_cast, ("req", "tp"), axis=0, tiled=True),
        lax.all_gather(k_cast, ("req", "tp"), axis=0, tiled=True),
        lax.all_gather(v_cast, ("req", "tp"), axis=0, tiled=True),
        lax.all_gather(o_cast, ("req", "tp"), axis=0, tiled=True),
        lax.all_gather(gate_cast, ("req", "tp"), axis=0, tiled=True),
        lax.all_gather(up_cast, ("req", "tp"), axis=0, tiled=True),
        lax.all_gather(down_cast, ("req", "tp"), axis=0, tiled=True),
    )
    query_weight = lax.dynamic_slice_in_dim(q_full, tensor_shard_index * q_cols, q_cols, 1)
    gate_weight = lax.dynamic_slice_in_dim(gate_full, tensor_shard_index * ff_cols, ff_cols, 1)
    up_weight = lax.dynamic_slice_in_dim(up_full, tensor_shard_index * ff_cols, ff_cols, 1)
    out_weight = lax.dynamic_slice_in_dim(o_full, tensor_shard_index * q_cols, q_cols, 0)
    down_weight = lax.dynamic_slice_in_dim(down_full, tensor_shard_index * ff_cols, ff_cols, 0)
    prompt_batch, sequence_length, model_width = hidden_in.shape
    tok_rows = prompt_batch * sequence_length
    flat_rows = hidden_in.reshape(tok_rows, model_width).astype(jnp.float32)
    normalized_input = rms_norm(flat_rows, attn_gain)
    local_heads = query_weight.shape[1] // HEAD_DIM
    queries = jnp.dot(normalized_input, query_weight, preferred_element_type=jnp.float32).reshape(
        prompt_batch, sequence_length, local_heads, HEAD_DIM
    )
    key_rows = jnp.dot(normalized_input, key_weight, preferred_element_type=jnp.float32).reshape(
        prompt_batch, sequence_length, KEY_VALUE_HEADS, HEAD_DIM
    )
    value_rows = jnp.dot(
        normalized_input, value_weight, preferred_element_type=jnp.float32
    ).reshape(prompt_batch, sequence_length, KEY_VALUE_HEADS, HEAD_DIM)
    cosine_table, sine_table = rope_tables(sequence_length, HEAD_DIM)
    q_rot = rotate(queries, cosine_table, sine_table).astype(jnp.bfloat16)
    rotated_keys = rotate(key_rows, cosine_table, sine_table).astype(jnp.bfloat16)
    value_halves = value_rows.astype(jnp.bfloat16)
    kv_cache = jnp.concatenate(
        [
            rotated_keys.reshape(prompt_batch, sequence_length, KEY_VALUE_HEADS * HEAD_DIM),
            value_halves.reshape(prompt_batch, sequence_length, KEY_VALUE_HEADS * HEAD_DIM),
        ],
        axis=2,
    )
    owner_shards = (
        tensor_shard_index * local_heads + jnp.arange(local_heads, dtype=jnp.int32)
    ) // (QUERY_HEADS // KEY_VALUE_HEADS)
    selector_mask = (
        owner_shards[:, None] == jnp.arange(KEY_VALUE_HEADS, dtype=jnp.int32)[None, :]
    ).astype(jnp.bfloat16)
    k_local = jnp.einsum(
        "pshd,gh->psgd", rotated_keys, selector_mask, preferred_element_type=jnp.float32
    ).astype(jnp.bfloat16)
    v_local = jnp.einsum(
        "pshd,gh->psgd", value_halves, selector_mask, preferred_element_type=jnp.float32
    ).astype(jnp.bfloat16)
    scores = jnp.einsum(
        "pqhd,pkhd->phqk", q_rot, k_local, preferred_element_type=jnp.float32
    ) / math.sqrt(HEAD_DIM)
    row_index = jnp.arange(sequence_length, dtype=jnp.int32)[:, None]
    col_index = jnp.arange(sequence_length, dtype=jnp.int32)[None, :]
    allowed = (col_index <= row_index)[None, None] & (
        col_index[None, None] < lengths[:, None, None, None]
    )
    scores = jnp.where(allowed, scores, -1e30)
    highest = jnp.max(scores, axis=-1, keepdims=True)
    expo = jnp.exp(scores - highest)
    weight_table = (expo / jnp.sum(expo, axis=-1, keepdims=True)).astype(jnp.bfloat16)
    attended = (
        jnp.einsum("phqk,pkhd->pqhd", weight_table, v_local, preferred_element_type=jnp.float32)
        .astype(jnp.bfloat16)
        .reshape(tok_rows, local_heads * HEAD_DIM)
    )
    attn_total = lax.psum(
        jnp.dot(attended, out_weight, preferred_element_type=jnp.float32).astype(jnp.bfloat16), "tp"
    ).astype(jnp.float32)
    middle = flat_rows + attn_total
    normed_rows = rms_norm(middle, mlp_gain)
    gate_val = jnp.dot(normed_rows, gate_weight, preferred_element_type=jnp.float32)
    up_val = jnp.dot(normed_rows, up_weight, preferred_element_type=jnp.float32)
    hidden_ff = (jax.nn.silu(gate_val) * up_val).astype(jnp.bfloat16)
    ffn_total = lax.psum(
        jnp.dot(hidden_ff, down_weight, preferred_element_type=jnp.float32).astype(jnp.bfloat16),
        "tp",
    ).astype(jnp.float32)
    result = (middle + ffn_total).astype(jnp.bfloat16)
    return (result.reshape(prompt_batch, sequence_length, model_width), kv_cache)


def solution(mesh):
    placed = (
        P("req", None, None),
        P("req"),
        P(),
        P(),
        P(("req", "tp"), None),
        P(("req", "tp"), None),
        P(("req", "tp"), None),
        P(("req", "tp"), None),
        P(("req", "tp"), None),
        P(("req", "tp"), None),
        P(("req", "tp"), None),
    )
    return jax.shard_map(
        local,
        mesh=mesh,
        in_specs=placed,
        out_specs=(P("req", None, None), P("req", None, None)),
        check_vma=False,
    )
```

profile of v0, /device:TPU:1, one launch (start us, length us, event | category | flops | bytes accessed | tf_op | source)
XLA Modules:
  0.0 559.3 jit_solution(9580003336960143405)
XLA Ops:
  7.2 1.5 convert_bitcast_fusion.4
  8.8 1.5 convert_bitcast_fusion.3
  10.4 0.7 convert_bitcast_fusion.5
  11.1 40.0 %all-gather.2 = bf16[128,10,320]{2,1,0:T(8,128)(2,1)S(1)} all-gather(bf16[1,10,320]{2,1,0:T(8,128)(2,1)S(1)} %convert_bitcast_fusion.5), channel_id=1, replica_groups=mesh['req'=32,'tp'=4] {'req','tp'}, dimensions={0}, use_global_device_ids=true | all-gather | bytes 825600 | tf_op jit(solution)/shard_map/all_gather | solution.py:66
  51.1 1.4 reshape.191
  52.5 1.7 copy.29
  54.2 37.9 %all-gather = bf16[128,10,320]{2,1,0:T(8,128)(2,1)} all-gather(bf16[1,10,320]{2,1,0:T(8,128)(2,1)S(1)} %convert_bitcast_fusion.6), channel_id=1, replica_groups=mesh['req'=32,'tp'=4] {'req','tp'}, dimensions={0}, use_global_device_ids=true | all-gather | bytes 825600 | tf_op jit(solution)/shard_map/all_gather | solution.py:67
  92.1 3.2 reshape.187
  95.3 2.2 copy.26
  97.6 0.6 multiply_reduce_fusion.1
  98.2 0.3 fusion.35
  98.5 1.1 fusion.29
  100.0 1.1 broadcast_and_fusion
  101.2 1.5 fusion.15
  102.7 1.2 convolution_convert_fusion.4
  103.9 0.9 copy-done.2
  104.8 1.5 fusion.14
  106.3 7.1 %reshape.189 = bf16[1280,1280]{1,0:T(8,128)(2,1)} reshape(bf16[128,10,1280]{2,1,0:T(8,128)(2,1)} %all-gather.13.cloned.1.call-done) | data formatting | bytes 6553600
  113.4 2.7 dynamic-slice_bitcast_fusion
  116.1 2.2 copy.28
  118.3 2.3 fusion.31
  120.7 1.1 subtract_convert_fusion
  121.7 9.6 %fusion.54 = (f32[2,5,512]{2,1,0:T(8,128)S(1)}, f32[2,5,512,512]{2,3,1,0:T(8,128)}) fusion(pred[2,512,512]{1,2,0:T(8,128)(4,1)} %broadcast_and_fusion, bf16[2,512,5,32]{1,3,2,0:T(8,128)(2,1)} %get-tuple-element.5, bf16[2,512,5,32]{1,3,2,0:T(8,128)(2,1)} %get-tuple-element.4, bf16[2,512,5,64]{1,2,3,0:T(8,128)(2,1)} %fusion.15), kind=kOutput, calls=%fused_computation.82 | convolution fusion | flops 347341312 | bytes 12341248 | tf_op jit(solution)/shard_map/sub | solution.py:125
  131.4 5.8 %fusion.17 = bf16[2,512,5,64]{1,3,2,0:T(8,128)(2,1)S(1)} fusion(f32[2,5,512,512]{2,3,1,0:T(8,128)} %get-tuple-element.9, f32[2,5,512]{2,1,0:T(8,128)S(1)} %get-tuple-element.8, bf16[2,512,5,64]{1,2,3,0:T(8,128)(2,1)} %fusion.14), kind=kOutput, calls=%fused_computation.32 | convolution fusion | flops 341114880 | bytes 11816960 | tf_op jit(solution)/shard_map/phqk,pkhd->pqhd/dot_general | solution.py:128
  137.1 0.7 copy.34
  137.8 0.9 copy.40
  138.7 11.3 %all-gather.15.cloned.1.call-done = bf16[128,10,1280]{2,1,0:T(8,128)(2,1)} async-done(((bf16[1,10,1280]{2,1,0:T(8,128)(2,1)}), bf16[128,10,1280]{2,1,0:T(8,128)(2,1)}) %all-gather.15.cloned.1.call-update) | async-done | bytes 3276816 | tf_op jit(solution)/shard_map/all_gather | solution.py:68
  150.1 7.0 %reshape.193 = bf16[1280,1280]{1,0:T(8,128)(2,1)} reshape(bf16[128,10,1280]{2,1,0:T(8,128)(2,1)} %all-gather.15.cloned.1.call-done) | data formatting | bytes 6553600
  157.1 4.4 convolution_convert_fusion.1
  161.7 0.7 convert_bitcast_fusion
  162.4 1.6 convert_bitcast_fusion.1
  164.1 1.6 convert_bitcast_fusion.2
  165.7 59.4 %all-reduce.3.cloned.1.call-done = bf16[1024,1280]{1,0:T(8,128)(2,1)} async-done(((bf16[1024,1280]{1,0:T(8,128)(2,1)}), bf16[1024,1280]{1,0:T(8,128)(2,1)}) %all-reduce.3.cloned.1.call-update) | async-done | bytes 2621456 | tf_op jit(solution)/shard_map/psum | solution.py:132
  225.1 2.8 multiply_reduce_fusion
  227.9 2.5 multiply_convert_fusion
  230.4 75.7 %all-gather.19.cloned.1.call-done = bf16[128,10,3584]{2,1,0:T(8,128)(2,1)} async-done(((bf16[1,10,3584]{2,1,0:T(8,128)(2,1)}), bf16[128,10,3584]{2,1,0:T(8,128)(2,1)}) %all-gather.19.cloned.1.call-update) | async-done | bytes 9175056 | tf_op jit(solution)/shard_map/all_gather | solution.py:70
  306.1 14.6 %reshape.197 = bf16[1280,3584]{1,0:T(8,128)(2,1)} reshape(bf16[128,10,3584]{2,1,0:T(8,128)(2,1)} %all-gather.19.cloned.1.call-done) | data formatting | bytes 18350080
  320.7 64.4 %all-gather.17.cloned.1.call-done = bf16[128,10,3584]{2,1,0:T(8,128)(2,1)} async-done(((bf16[1,10,3584]{2,1,0:T(8,128)(2,1)}), bf16[128,10,3584]{2,1,0:T(8,128)(2,1)}) %all-gather.17.cloned.1.call-update) | async-done | bytes 9175056 | tf_op jit(solution)/shard_map/all_gather | solution.py:69
  385.1 14.7 %reshape.195 = bf16[1280,3584]{1,0:T(8,128)(2,1)} reshape(bf16[128,10,3584]{2,1,0:T(8,128)(2,1)} %all-gather.17.cloned.1.call-done) | data formatting | bytes 18350080
  399.7 7.1 %fusion.8 = f32[1024,896]{1,0:T(8,128)} fusion(bf16[1024,1280]{1,0:T(8,128)(2,1)} %multiply_convert_fusion, bf16[1280,3584]{1,0:T(8,128)(2,1)} %reshape.197, s32[]{:T(128)S(6)} %select_n.25), kind=kOutput, calls=%fused_computation.20 | convolution fusion | flops 2348810240 | bytes 8585220 | tf_op jit(solution)/shard_map/dot_general | solution.py:138
  406.9 52.1 %all-gather.21.cloned.1.call-done = bf16[128,28,1280]{2,1,0:T(8,128)(2,1)} async-done(((bf16[1,28,1280]{2,1,0:T(8,128)(2,1)}), bf16[128,28,1280]{2,1,0:T(8,128)(2,1)}) %all-gather.21.cloned.1.call-update) | async-done | bytes 9175056 | tf_op jit(solution)/shard_map/all_gather | solution.py:71
  459.0 13.1 %reshape.199 = bf16[3584,1280]{1,0:T(8,128)(2,1)} reshape(bf16[128,28,1280]{2,1,0:T(8,128)(2,1)} %all-gather.21.cloned.1.call-done) | data formatting | bytes 18350080
  472.1 11.5 %convolution_convert_fusion = bf16[1024,1280]{1,0:T(8,128)(2,1)} fusion(bf16[3584,1280]{1,0:T(8,128)(2,1)} %reshape.199, s32[]{:T(128)S(6)} %select_n.25, f32[1024,896]{1,0:T(8,128)} %fusion.8, bf16[1024,1280]{1,0:T(8,128)(2,1)} %multiply_convert_fusion, bf16[1280,3584]{1,0:T(8,128)(2,1)} %reshape.195), kind=kOutput, calls=%fused_computation.15 | convolution fusion | flops 4704436224 | bytes 13501440 | tf_op jit(solution)/shard_map/dot_general | solution.py:141
  483.6 1.2 copy.35
  484.7 1.4 copy.36
  486.2 2.6 pad_maximum_fusion
  488.8 58.7 %all-reduce.5.cloned.1.call-done = bf16[1024,1280]{1,0:T(8,128)(2,1)} async-done(((bf16[1024,1280]{1,0:T(8,128)(2,1)}), bf16[1024,1280]{1,0:T(8,128)(2,1)}) %all-reduce.5.cloned.1.call-update) | async-done | bytes 2621456 | tf_op jit(solution)/shard_map/psum | solution.py:140
  547.5 5.0 add_convert_fusion
  (45 shorter events, 0.9 us)
Async XLA Ops:
  7.2 47.0 %copy-start.7 = (f32[10,320]{1,0:T(8,128)S(1)}, f32[10,320]{1,0:T(8,128)}, u32[]{:S(2)}) copy-start(f32[10,320]{1,0:T(8,128)} %param.17) | copy-start | bytes 38404
  7.2 99.1 %all-gather.13.cloned.1.call-start = ((), (), s32[]{:S(2)}) async-start(), calls=%async_computation.2 | async-start | bytes 5283840 | tf_op jit(solution)/shard_map/all_gather | solution.py:65
  8.7 141.4 %all-gather.15.cloned.1.call-start = ((), (), s32[]{:S(2)}) async-start(), calls=%async_computation.3 | async-start | bytes 5283840 | tf_op jit(solution)/shard_map/all_gather | solution.py:68
  10.3 214.8 %all-reduce.3.cloned.1.call-start = ((), (), s32[]{:S(2)}) async-start(), calls=%async_computation | async-start | bytes 5242880 | tf_op jit(solution)/shard_map/psum | solution.py:132
  52.5 45.1 %copy-start = (bf16[2,512,1280]{2,1,0:T(8,128)(2,1)S(1)}, bf16[2,512,1280]{2,1,0:T(8,128)(2,1)}, u32[]{:S(2)}) copy-start(bf16[2,512,1280]{2,1,0:T(8,128)(2,1)} %param.11) | copy-start | bytes 7864324
  92.1 6.5 %copy-start.10 = (f32[1280]{0:T(1024)S(1)}, f32[1280]{0:T(1024)}, u32[]{:S(2)}) copy-start(f32[1280]{0:T(1024)} %param.13) | copy-start | bytes 15364
  98.5 1.2 copy-start.4
  98.5 1.4 copy-start.9
  99.7 3.1 copy-start.3
  103.9 0.9 copy-start.2
  118.3 2.3 copy-start.5
  157.1 4.5 copy-start.6
  161.6 66.3 %copy-start.8 = (f32[1280]{0:T(1024)S(1)}, f32[1280]{0:T(1024)}, u32[]{:S(2)}) copy-start(f32[1280]{0:T(1024)} %param.14) | copy-start | bytes 15364
  161.6 144.5 %all-gather.19.cloned.1.call-start = ((), (), s32[]{:S(2)}) async-start(), calls=%async_computation.5 | async-start | bytes 14794752 | tf_op jit(solution)/shard_map/all_gather | solution.py:70
  162.3 222.7 %all-gather.17.cloned.1.call-start = ((), (), s32[]{:S(2)}) async-start(), calls=%async_computation.4 | async-start | bytes 14794752 | tf_op jit(solution)/shard_map/all_gather | solution.py:69
  164.0 295.0 %all-gather.21.cloned.1.call-start = ((), (), s32[]{:S(2)}) async-start(), calls=%async_computation.6 | async-start | bytes 10567680 | tf_op jit(solution)/shard_map/all_gather | solution.py:71
  165.6 381.8 %all-reduce.5.cloned.1.call-start = ((), (), s32[]{:S(2)}) async-start(), calls=%async_computation.1 | async-start | bytes 5242880 | tf_op jit(solution)/shard_map/psum | solution.py:140
  225.1 2.8 copy-start.1
Sparse Core Ops, SparseCore 0:
  11.0 71.2 all-gather.12
  85.2 64.8 all-gather.14
  161.7 63.3 all-reduce.2
  228.5 77.5 all-gather.18
  308.9 76.1 all-gather.16
  388.1 70.8 all-gather.20
  483.7 63.7 all-reduce.4
where the time goes:
time: 561 us; the launch traced here: 559 us
  waiting for transfers between devices  322 us (57%)
  blocking collectives  77.8 us (14%)
  local copies, waits for them, and re-layouts  75 us (13%)
  matrix products  46.1 us (8%)
  other arithmetic  24 us (4%)
  between operations  14.4 us (3%)
    all_gather x1, waiting for transfers between devices, local(): lax.all_gather(up_cast, ('req', 'tp'), axis=0, tiled=True)  75.7 us
    all_gather x1, waiting for transfers between devices, local(): lax.all_gather(gate_cast, ('req', 'tp'), axis=0, tiled=True)  64.4 us
    unnamed x30, local copies, waits for them, and re-layouts  62.9 us
    psum x1, waiting for transfers between devices, local(): lax.psum(jnp.dot(attended, out_weight, preferred_element_type=jnp.float32...  59.4 us
    psum x1, waiting for transfers between devices, local(): lax.psum(jnp.dot(hidden_ff, down_weight, preferred_element_type=jnp.float...  58.7 us
    all_gather x1, waiting for transfers between devices, local(): lax.all_gather(down_cast, ('req', 'tp'), axis=0, tiled=True)  52.1 us
    all_gather x1, blocking collectives, local(): lax.all_gather(k_cast, ('req', 'tp'), axis=0, tiled=True)  40 us
    all_gather x1, blocking collectives, local(): lax.all_gather(v_cast, ('req', 'tp'), axis=0, tiled=True)  37.9 us
  transfers between devices with their start and end apart: 7, of which 6 were waited for; matrix products, arithmetic and copies ran while one was open for 18% of the time, Pallas kernels for 0%

commit v1 on v0

--- a/solution.py
+++ b/solution.py
@@ -51,30 +51,54 @@
     down_master,
 ):
     tp_count = lax.axis_size("tp")
+    req_count = lax.axis_size("req")
     tensor_shard_index = lax.axis_index("tp")
-    q_cast = q_master.astype(jnp.bfloat16)
-    k_cast = k_master.astype(jnp.bfloat16)
-    v_cast = trainer_value_weight.astype(jnp.bfloat16)
-    o_cast = o_master.astype(jnp.bfloat16)
-    gate_cast = gate_master.astype(jnp.bfloat16)
-    up_cast = up_master.astype(jnp.bfloat16)
-    down_cast = down_master.astype(jnp.bfloat16)
+    bf = jnp.bfloat16
     q_cols = q_master.shape[1] // tp_count
+    kv_cols = k_master.shape[1]
     ff_cols = gate_master.shape[1] // tp_count
-    q_full, key_weight, value_weight, o_full, gate_full, up_full, down_full = (
-        lax.all_gather(q_cast, ("req", "tp"), axis=0, tiled=True),
-        lax.all_gather(k_cast, ("req", "tp"), axis=0, tiled=True),
-        lax.all_gather(v_cast, ("req", "tp"), axis=0, tiled=True),
-        lax.all_gather(o_cast, ("req", "tp"), axis=0, tiled=True),
-        lax.all_gather(gate_cast, ("req", "tp"), axis=0, tiled=True),
-        lax.all_gather(up_cast, ("req", "tp"), axis=0, tiled=True),
-        lax.all_gather(down_cast, ("req", "tp"), axis=0, tiled=True),
-    )
-    query_weight = lax.dynamic_slice_in_dim(q_full, tensor_shard_index * q_cols, q_cols, 1)
-    gate_weight = lax.dynamic_slice_in_dim(gate_full, tensor_shard_index * ff_cols, ff_cols, 1)
-    up_weight = lax.dynamic_slice_in_dim(up_full, tensor_shard_index * ff_cols, ff_cols, 1)
-    out_weight = lax.dynamic_slice_in_dim(o_full, tensor_shard_index * q_cols, q_cols, 0)
-    down_weight = lax.dynamic_slice_in_dim(down_full, tensor_shard_index * ff_cols, ff_cols, 0)
+    local_rows = q_master.shape[0]
+
+    def dest_chunk(dest):
+        return jnp.concatenate(
+            [
+                q_master[:, dest * q_cols : (dest + 1) * q_cols],
+                k_master,
+                trainer_value_weight,
+                gate_master[:, dest * ff_cols : (dest + 1) * ff_cols],
+                up_master[:, dest * ff_cols : (dest + 1) * ff_cols],
+            ],
+            axis=1,
+        ).astype(bf)
+
+    send = jnp.stack([dest_chunk(d) for d in range(tp_count)])
+    recv = lax.all_to_all(send, "tp", 0, 0, tiled=False)
+    col_block = recv.reshape(tp_count * local_rows, -1)
+
+    row_pack = jnp.concatenate([o_master.reshape(-1), down_master.reshape(-1)]).astype(bf)
+    per_block = req_count // tp_count
+    perm = []
+    for r_src in range(req_count):
+        for t_src in range(tp_count):
+            r_dst = tp_count * (r_src % per_block) + t_src
+            t_dst = r_src // per_block
+            perm.append((r_src * tp_count + t_src, r_dst * tp_count + t_dst))
+    row_pack = lax.ppermute(row_pack, ("req", "tp"), perm)
+
+    packed = jnp.concatenate([col_block.reshape(-1), row_pack])
+    gathered = lax.all_gather(packed, "req", axis=0, tiled=False)
+    col_size = col_block.size
+    all_cols = gathered[:, :col_size].reshape(-1, col_block.shape[1])
+    offs = [0, q_cols, q_cols + kv_cols, q_cols + 2 * kv_cols, q_cols + 2 * kv_cols + ff_cols]
+    query_weight = all_cols[:, offs[0] : offs[1]]
+    key_weight = all_cols[:, offs[1] : offs[2]]
+    value_weight = all_cols[:, offs[2] : offs[3]]
+    gate_weight = all_cols[:, offs[3] : offs[4]]
+    up_weight = all_cols[:, offs[4] : offs[4] + ff_cols]
+    o_size = o_master.size
+    model_cols = o_master.shape[1]
+    out_weight = gathered[:, col_size : col_size + o_size].reshape(-1, model_cols)
+    down_weight = gathered[:, col_size + o_size :].reshape(-1, model_cols)
     prompt_batch, sequence_length, model_width = hidden_in.shape
     tok_rows = prompt_batch * sequence_length
     flat_rows = hidden_in.reshape(tok_rows, model_width).astype(jnp.float32)

time: 561 us -> 378 us (0.67)
  waiting for transfers between devices: 322 us -> 234 us
  blocking collectives: 77.8 us -> 0 us
  local copies, waits for them, and re-layouts: 75 us -> 53.4 us
  starting transfers between devices: 0.29 us -> 9.81 us
    all_gather x5 -> x1, waiting for transfers between devices: 204 us -> 117 us  [local(): gathered = lax.all_gather(packed, 'req', axis=0, tiled=False)]
    all_gather x2 -> x0, blocking collectives: 77.8 us -> none  [the longest x1 40 us: local(): lax.all_gather(k_cast, ('req', 'tp'), axis=0, tiled=True)]
    unnamed x30 -> x27, local copies, waits for them, and re-layouts: 62.9 us -> 1.78 us
    reshape x0 -> x5, local copies, waits for them, and re-layouts: none -> 17.8 us  [the longest x1 9.56 us: local(): all_cols = gathered[:, :col_size].reshape(-1, col_block.shape[1])]
    all_gather x0 -> x1, local copies, waits for them, and re-layouts: none -> 9.91 us  [local(): gathered = lax.all_gather(packed, 'req', axis=0, tiled=False)]
    slice x0 -> x4, local copies, waits for them, and re-layouts: none -> 9.67 us  [the longest x1 6.41 us: local(): all_cols = gathered[:, :col_size].reshape(-1, col_block.shape[1])]
    unnamed x7 -> x0, other arithmetic: 7.56 us -> none
  transfers between devices with their start and end apart: 7 -> 5, of which waited for: 6 -> 5; matrix products, arithmetic and copies ran while one was open for 18% -> 5% of each run, Pallas kernels for 0% -> 0%
where the time goes in v1:
time: 378 us; the launch traced here: 377 us
  waiting for transfers between devices  234 us (62%)
  local copies, waits for them, and re-layouts  53.4 us (14%)
  matrix products  44.6 us (12%)
  other arithmetic  21.1 us (6%)
  between operations  14 us (4%)
  starting transfers between devices  9.81 us (3%)
    all_gather x1, waiting for transfers between devices, local(): gathered = lax.all_gather(packed, 'req', axis=0, tiled=False)  117 us
    psum x1, waiting for transfers between devices, local(): lax.psum(jnp.dot(hidden_ff, down_weight, preferred_element_type=jnp.float...  60.5 us
    psum x1, waiting for transfers between devices, local(): lax.psum(jnp.dot(attended, out_weight, preferred_element_type=jnp.float32...  55.5 us
    dot_general x1, matrix products, local(): jnp.dot(hidden_ff, down_weight, preferred_element_type=jnp.float32)  11.6 us
    all_gather x1, local copies, waits for them, and re-layouts, local(): gathered = lax.all_gather(packed, 'req', axis=0, tiled=False)  9.91 us
    sub x1, matrix products, local(): expo = jnp.exp(scores - highest)  9.61 us
    reshape x1, local copies, waits for them, and re-layouts, local(): all_cols = gathered[:, :col_size].reshape(-1, col_block.shape[1])  9.56 us
  transfers between devices with their start and end apart: 5, of which 5 were waited for; matrix products, arithmetic and copies ran while one was open for 5% of the time, Pallas kernels for 0%

profile of v1, /device:TPU:1, one launch (start us, length us, event | category | flops | bytes accessed | tf_op | source)
XLA Modules:
  0.0 377.0 jit_solution(8309869732816319667)
XLA Ops:
  7.2 1.0 convert.69
  8.3 1.0 convert.72
  9.3 1.0 convert.73
  10.2 0.8 convert_bitcast_fusion
  11.5 0.8 pad_maximum_fusion.8
  12.3 4.8 %all-to-all-start = ((bf16[4,10,2752]{2,1,0:T(8,128)(2,1)}), bf16[4,10,2752]{2,1,0:T(8,128)(2,1)S(1)}, u32[]{:S(2)}, u32[]{:S(2)}) async-start(bf16[4,10,2752]{2,1,0:T(8,128)(2,1)} %pad_maximum_fusion.8), calls=%async_computation | async-start | bytes 720896 | tf_op jit(solution)/shard_map/all_to_all | solution.py:75
  17.4 4.9 %collective-permute-start = (bf16[48640]{0:T(1024)(128)(2,1)S(1)}, bf16[48640]{0:T(1024)(128)(2,1)S(1)}, u32[]{:S(2)}, u32[]{:S(2)}) collective-permute-start(bf16[48640]{0:T(1024)(128)(2,1)S(1)} %pad_maximum_fusion.10), channel_id=1, source_target_pairs={{0,0},{1,4},{2,8},{3,12},{4,16},{5,20},{6,24},{7,28},{8,32},{9,36}... | collective-permute-start | bytes 291848 | tf_op jit(solution)/shard_map/ppermute | solution.py:86
  22.3 0.9 all-to-all-done
  23.2 0.3 reshape_reshape.3
  23.5 0.4 collective-permute-done
  23.9 0.8 pad_maximum_fusion.9
  25.0 0.6 multiply_reduce_fusion.1
  25.6 0.9 fusion.36
  26.5 1.1 broadcast_and_fusion
  27.7 116.6 %all-gather.3.cloned.1.call-done = bf16[5079040]{0:T(1024)(128)(2,1)} async-done(((bf16[158720]{0:T(1024)(128)(2,1)}), bf16[5079040]{0:T(1024)(128)(2,1)}) %all-gather.3.cloned.1.call-update) | async-done | bytes 10158096 | tf_op jit(solution)/shard_map/all_gather | solution.py:89
  144.3 9.9 %reshape.494 = bf16[32,158720]{1,0:T(8,128)(2,1)} reshape(bf16[5079040]{0:T(1024)(128)(2,1)} %all-gather.3.cloned.1.call-done) | data formatting | bytes 20316160 | tf_op jit(solution)/shard_map/all_gather | solution.py:89
  154.2 6.4 %slice.120 = bf16[32,110080]{1,0:T(8,128)(2,1)} slice(bf16[32,158720]{1,0:T(8,128)(2,1)} %reshape.494), slice={[0:32], [0:110080]} | slice | bytes 14090240 | tf_op jit(solution)/shard_map/slice | solution.py:91
  160.6 2.1 reshape.487
  162.7 9.6 %reshape.485 = bf16[1280,2752]{1,0:T(8,128)(2,1)} reshape(bf16[32,110080]{1,0:T(8,128)(2,1)} %slice.120) | data formatting | bytes 14090240 | tf_op jit(solution)/shard_map/reshape | solution.py:91
  172.3 4.0 %slice_bitcast_fusion.2 = (bf16[320,1280]{0,1:T(8,128)(2,1)}, bf16[320,1280]{0,1:T(8,128)(2,1)}, bf16[320,1280]{0,1:T(8,128)(2,1)}) fusion(bf16[1280,2752]{1,0:T(8,128)(2,1)} %reshape.485), kind=kLoop, calls=%fused_computation.40 | loop fusion | bytes 4915200 | tf_op jit(solution)/shard_map/dot_general | solution.py:113
  176.3 1.5 copy.23
  177.8 2.2 copy.26
  180.0 2.0 convolution_convert_fusion.4
  182.0 2.2 fusion.30
  184.2 1.7 copy.25
  185.9 1.1 fusion.32
  187.0 0.2 copy-done.4
  187.2 0.2 multiply_subtract_fusion
  187.4 1.1 subtract_convert_fusion
  188.5 1.5 fusion.17
  190.1 1.5 fusion.16
  191.6 9.6 %fusion.49 = (f32[2,5,512]{2,1,0:T(8,128)S(1)}, f32[2,5,512,512]{2,3,1,0:T(8,128)}) fusion(pred[2,512,512]{1,2,0:T(8,128)(4,1)} %broadcast_and_fusion, bf16[2,512,5,32]{1,3,2,0:T(8,128)(2,1)} %get-tuple-element.8, bf16[2,512,5,32]{1,3,2,0:T(8,128)(2,1)} %get-tuple-element.7, bf16[2,512,5,64]{1,2,3,0:T(8,128)(2,1)} %fusion.17), kind=kOutput, calls=%fused_computation.89 | convolution fusion | flops 347341312 | bytes 12341248 | tf_op jit(solution)/shard_map/sub | solution.py:149
  201.2 5.4 %fusion.19 = bf16[2,512,5,64]{1,3,2,0:T(8,128)(2,1)S(1)} fusion(f32[2,5,512,512]{2,3,1,0:T(8,128)} %get-tuple-element.24, f32[2,5,512]{2,1,0:T(8,128)S(1)} %get-tuple-element.23, bf16[2,512,5,64]{1,2,3,0:T(8,128)(2,1)} %fusion.16), kind=kOutput, calls=%fused_computation.32 | convolution fusion | flops 341114880 | bytes 11816960 | tf_op jit(solution)/shard_map/phqk,pkhd->pqhd/dot_general | solution.py:152
  206.6 0.7 copy.31
  207.4 3.1 convolution_convert_fusion.1
  210.6 3.3 slice.131
  213.8 5.9 %reshape.488 = bf16[896,1280]{1,0:T(8,128)(2,1)} reshape(bf16[32,35840]{1,0:T(8,128)(2,1)} %slice.131) | data formatting | bytes 4587520 | tf_op jit(solution)/shard_map/reshape | solution.py:101
  219.7 55.5 %all-reduce.3.cloned.1.call-done = bf16[1024,1280]{1,0:T(8,128)(2,1)} async-done(((bf16[1024,1280]{1,0:T(8,128)(2,1)}), bf16[1024,1280]{1,0:T(8,128)(2,1)}) %all-reduce.3.cloned.1.call-update) | async-done | bytes 2621456 | tf_op jit(solution)/shard_map/psum | solution.py:156
  275.2 2.8 multiply_reduce_fusion
  278.1 1.0 multiply_convert_fusion
  279.1 1.5 copy-done.3
  280.6 6.5 %fusion.7 = f32[1024,896]{1,0:T(8,128)} fusion(bf16[1024,1280]{1,0:T(8,128)(2,1)S(1)} %multiply_convert_fusion, bf16[1280,2752]{1,0:T(8,128)(2,1)} %reshape.485), kind=kOutput, calls=%fused_computation.19 | convolution fusion | flops 2348810240 | bytes 8585216 | tf_op jit(solution)/shard_map/dot_general | solution.py:162
  287.1 11.6 %convolution_convert_fusion = bf16[1024,1280]{1,0:T(8,128)(2,1)} fusion(bf16[896,1280]{1,0:T(8,128)(2,1)} %reshape.488, f32[1024,896]{1,0:T(8,128)} %fusion.7, bf16[1024,1280]{1,0:T(8,128)(2,1)} %copy-done.3, bf16[1280,2752]{1,0:T(8,128)(2,1)} %reshape.485), kind=kOutput, calls=%fused_computation.15 | convolution fusion | flops 4704436224 | bytes 13500416 | tf_op jit(solution)/shard_map/dot_general | solution.py:165
  298.7 2.2 copy.33
  301.0 1.2 copy.32
  302.1 2.8 pad_maximum_fusion
  305.0 60.5 %all-reduce.5.cloned.1.call-done = bf16[1024,1280]{1,0:T(8,128)(2,1)} async-done(((bf16[1024,1280]{1,0:T(8,128)(2,1)}), bf16[1024,1280]{1,0:T(8,128)(2,1)}) %all-reduce.5.cloned.1.call-update) | async-done | bytes 2621456 | tf_op jit(solution)/shard_map/psum | solution.py:164
  365.5 5.0 %add_convert_fusion = bf16[1024,1280]{1,0:T(8,128)(2,1)} fusion(bf16[1024,1280]{1,0:T(8,128)(2,1)} %all-reduce.5.cloned.1.call-done, bf16[1024,1280]{1,0:T(8,128)(2,1)} %all-reduce.3.cloned.1.call-done, bf16[2,512,1280]{2,1,0:T(8,128)(2,1)S(1)} %copy-done), kind=kLoop, calls=%fused_computation.6 | loop fusion | flops 7864320 | bytes 10485760 | tf_op jit(solution)/shard_map/convert_element_type | solution.py:168
  (51 shorter events, 1.3 us)
Async XLA Ops:
  7.2 10.0 %copy-start.9 = (f32[10,1280]{1,0:T(8,128)S(1)}, f32[10,1280]{1,0:T(8,128)}, u32[]{:S(2)}) copy-start(f32[10,1280]{1,0:T(8,128)} %param.18) | copy-start | bytes 153604
  7.2 10.0 %copy-start.8 = (f32[28,1280]{1,0:T(8,128)S(1)}, f32[28,1280]{1,0:T(8,128)}, u32[]{:S(2)}) copy-start(f32[28,1280]{1,0:T(8,128)} %param.21) | copy-start | bytes 430084
  7.2 17.7 %copy-start.11 = (s32[2]{0:T(128)S(1)}, s32[2]{0:T(128)}, u32[]{:S(2)}) copy-start(s32[2]{0:T(128)} %param.12) | copy-start | bytes 28
  7.2 17.8 %copy-start = (bf16[2,512,1280]{2,1,0:T(8,128)(2,1)S(1)}, bf16[2,512,1280]{2,1,0:T(8,128)(2,1)}, u32[]{:S(2)}) copy-start(bf16[2,512,1280]{2,1,0:T(8,128)(2,1)} %param.11) | copy-start | bytes 7864324
  12.3 10.9 %all-to-all-start = ((bf16[4,10,2752]{2,1,0:T(8,128)(2,1)}), bf16[4,10,2752]{2,1,0:T(8,128)(2,1)S(1)}, u32[]{:S(2)}, u32[]{:S(2)}) async-start(bf16[4,10,2752]{2,1,0:T(8,128)(2,1)} %pad_maximum_fusion.8), calls=%async_computation | async-start | bytes 720896 | tf_op jit(solution)/shard_map/all_to_all | solution.py:75
  17.1 127.2 %all-gather.3.cloned.1.call-start = ((), (), s32[]{:S(2)}) async-start(), calls=%async_computation.3 | async-start | bytes 10475520 | tf_op jit(solution)/shard_map/all_gather | solution.py:89
  17.4 6.5 %collective-permute-start = (bf16[48640]{0:T(1024)(128)(2,1)S(1)}, bf16[48640]{0:T(1024)(128)(2,1)S(1)}, u32[]{:S(2)}, u32[]{:S(2)}) collective-permute-start(bf16[48640]{0:T(1024)(128)(2,1)S(1)} %pad_maximum_fusion.10), channel_id=1, source_target_pairs={{0,0},{1,4},{2,8},{3,12},{4,16},{5,20},{6,24},{7,28},{8,32},{9,36}... | collective-permute-start | bytes 291848 | tf_op jit(solution)/shard_map/ppermute | solution.py:86
  24.7 250.5 %all-reduce.3.cloned.1.call-start = ((), (), s32[]{:S(2)}) async-start(), calls=%async_computation.1 | async-start | bytes 5242880 | tf_op jit(solution)/shard_map/psum | solution.py:156
  154.2 6.4 %slice-start = ((bf16[32,158720]{1,0:T(8,128)(2,1)}), bf16[32,12800]{1,0:T(8,128)(2,1)S(1)}, s32[]{:S(2)}) async-start(bf16[32,158720]{1,0:T(8,128)(2,1)} %reshape.494), calls=%async_computation.4 | async-start | bytes 1638400 | tf_op jit(solution)/shard_map/slice | solution.py:100
  172.3 7.7 %copy-start.12 = (f32[1280]{0:T(1024)S(1)}, f32[1280]{0:T(1024)}, u32[]{:S(2)}) copy-start(f32[1280]{0:T(1024)} %param.13) | copy-start | bytes 15364
  180.0 2.0 copy-start.5
  185.9 1.3 copy-start.4
  185.9 1.3 copy-start.7
  187.2 2.9 copy-start.2
  201.2 6.2 %copy-start.6 = (bf16[320,1280]{1,0:T(8,128)(2,1)S(1)}, bf16[320,1280]{1,0:T(8,128)(2,1)}, u32[]{:S(2)}) copy-start(bf16[320,1280]{1,0:T(8,128)(2,1)} %reshape.487) | copy-start | bytes 2457604
  210.5 155.0 %all-reduce.5.cloned.1.call-start = ((), (), s32[]{:S(2)}) async-start(), calls=%async_computation.2 | async-start | bytes 5242880 | tf_op jit(solution)/shard_map/psum | solution.py:164
  219.7 58.4 %copy-start.10 = (f32[1280]{0:T(1024)S(1)}, f32[1280]{0:T(1024)}, u32[]{:S(2)}) copy-start(f32[1280]{0:T(1024)} %param.14) | copy-start | bytes 15364
  275.2 2.8 copy-start.1
  279.1 1.5 copy-start.3
Sparse Core Ops, SparseCore 0:
  24.8 119.4 all-gather.2
  210.6 64.5 all-reduce.2
  298.9 66.5 all-reduce.4

commit v2 on v1

--- a/solution.py
+++ b/solution.py
@@ -34,6 +34,40 @@
     return jnp.concatenate(
         [first_half * cos_b - second_half * sin_b, second_half * cos_b + first_half * sin_b],
         axis=-1,
+    )
+
+
+CHIP_PAIRS = [(0, 1), (1, 0), (2, 3), (3, 2)]
+CROSS_PAIRS = [(0, 2), (2, 0), (1, 3), (3, 1)]
+
+
+def pick(stack, index):
+    return lax.dynamic_index_in_dim(stack, index, axis=0, keepdims=False)
+
+
+def tp_reduce_scatter(partial, core_bit, chip_bit):
+    rows, width = partial.shape
+    halves = partial.reshape(2, rows // 2, width)
+    got = lax.ppermute(pick(halves, 1 - core_bit), "tp", CHIP_PAIRS)
+    first = pick(halves, core_bit).astype(jnp.float32) + got.astype(jnp.float32)
+    quarters = first.reshape(2, rows // 4, width)
+    sent = pick(quarters, 1 - chip_bit).astype(jnp.bfloat16)
+    got = lax.ppermute(sent, "tp", CROSS_PAIRS)
+    return pick(quarters, chip_bit) + got.astype(jnp.float32)
+
+
+def tp_all_gather(quarter, core_bit, chip_bit):
+    got = lax.ppermute(quarter, "tp", CROSS_PAIRS)
+    half = jnp.where(
+        chip_bit == 0,
+        jnp.concatenate([quarter, got], axis=0),
+        jnp.concatenate([got, quarter], axis=0),
+    )
+    got = lax.ppermute(half, "tp", CHIP_PAIRS)
+    return jnp.where(
+        core_bit == 0,
+        jnp.concatenate([half, got], axis=0),
+        jnp.concatenate([got, half], axis=0),
     )
 
 
@@ -53,11 +87,15 @@
     tp_count = lax.axis_size("tp")
     req_count = lax.axis_size("req")
     tensor_shard_index = lax.axis_index("tp")
+    core_bit = tensor_shard_index % 2
+    chip_bit = tensor_shard_index // 2
     bf = jnp.bfloat16
     q_cols = q_master.shape[1] // tp_count
     kv_cols = k_master.shape[1]
     ff_cols = gate_master.shape[1] // tp_count
     local_rows = q_master.shape[0]
+    model_cols = o_master.shape[1]
+    block_rows = tp_count * local_rows
 
     def dest_chunk(dest):
         return jnp.concatenate(
@@ -73,8 +111,10 @@
 
     send = jnp.stack([dest_chunk(d) for d in range(tp_count)])
     recv = lax.all_to_all(send, "tp", 0, 0, tiled=False)
-    col_block = recv.reshape(tp_count * local_rows, -1)
-
+    col_block = recv.reshape(block_rows, -1)
+    qkv_width = q_cols + 2 * kv_cols
+
+    o_size = o_master.size
     row_pack = jnp.concatenate([o_master.reshape(-1), down_master.reshape(-1)]).astype(bf)
     per_block = req_count // tp_count
     perm = []
@@ -85,34 +125,32 @@
             perm.append((r_src * tp_count + t_src, r_dst * tp_count + t_dst))
     row_pack = lax.ppermute(row_pack, ("req", "tp"), perm)
 
-    packed = jnp.concatenate([col_block.reshape(-1), row_pack])
-    gathered = lax.all_gather(packed, "req", axis=0, tiled=False)
-    col_size = col_block.size
-    all_cols = gathered[:, :col_size].reshape(-1, col_block.shape[1])
-    offs = [0, q_cols, q_cols + kv_cols, q_cols + 2 * kv_cols, q_cols + 2 * kv_cols + ff_cols]
-    query_weight = all_cols[:, offs[0] : offs[1]]
-    key_weight = all_cols[:, offs[1] : offs[2]]
-    value_weight = all_cols[:, offs[2] : offs[3]]
-    gate_weight = all_cols[:, offs[3] : offs[4]]
-    up_weight = all_cols[:, offs[4] : offs[4] + ff_cols]
-    o_size = o_master.size
-    model_cols = o_master.shape[1]
-    out_weight = gathered[:, col_size : col_size + o_size].reshape(-1, model_cols)
-    down_weight = gathered[:, col_size + o_size :].reshape(-1, model_cols)
+    attn_pack = jnp.concatenate(
+        [col_block[:, :qkv_width], row_pack[:o_size].reshape(block_rows, -1)], axis=1
+    )
+    ffn_pack = jnp.concatenate(
+        [col_block[:, qkv_width:], row_pack[o_size:].reshape(block_rows, -1)], axis=1
+    )
+    attn_all = lax.all_gather(attn_pack, "req", axis=0, tiled=True)
+    ffn_all = lax.all_gather(ffn_pack, "req", axis=0, tiled=True)
+    qkv_weight = attn_all[:, :qkv_width]
+    out_weight = attn_all[:, qkv_width:].reshape(req_count, -1).reshape(-1, model_cols)
+    gate_up_weight = ffn_all[:, : 2 * ff_cols]
+    down_weight = ffn_all[:, 2 * ff_cols :].reshape(req_count, -1).reshape(-1, model_cols)
+
     prompt_batch, sequence_length, model_width = hidden_in.shape
     tok_rows = prompt_batch * sequence_length
     flat_rows = hidden_in.reshape(tok_rows, model_width).astype(jnp.float32)
     normalized_input = rms_norm(flat_rows, attn_gain)
-    local_heads = query_weight.shape[1] // HEAD_DIM
-    queries = jnp.dot(normalized_input, query_weight, preferred_element_type=jnp.float32).reshape(
-        prompt_batch, sequence_length, local_heads, HEAD_DIM
-    )
-    key_rows = jnp.dot(normalized_input, key_weight, preferred_element_type=jnp.float32).reshape(
+    local_heads = q_cols // HEAD_DIM
+    qkv = jnp.dot(normalized_input, qkv_weight, preferred_element_type=jnp.float32)
+    queries = qkv[:, :q_cols].reshape(prompt_batch, sequence_length, local_heads, HEAD_DIM)
+    key_rows = qkv[:, q_cols : q_cols + kv_cols].reshape(
         prompt_batch, sequence_length, KEY_VALUE_HEADS, HEAD_DIM
     )
-    value_rows = jnp.dot(
-        normalized_input, value_weight, preferred_element_type=jnp.float32
-    ).reshape(prompt_batch, sequence_length, KEY_VALUE_HEADS, HEAD_DIM)
+    value_rows = qkv[:, q_cols + kv_cols :].reshape(
+        prompt_batch, sequence_length, KEY_VALUE_HEADS, HEAD_DIM
+    )
     cosine_table, sine_table = rope_tables(sequence_length, HEAD_DIM)
     q_rot = rotate(queries, cosine_table, sine_table).astype(jnp.bfloat16)
     rotated_keys = rotate(key_rows, cosine_table, sine_table).astype(jnp.bfloat16)
@@ -153,19 +191,21 @@
         .astype(jnp.bfloat16)
         .reshape(tok_rows, local_heads * HEAD_DIM)
     )
-    attn_total = lax.psum(
-        jnp.dot(attended, out_weight, preferred_element_type=jnp.float32).astype(jnp.bfloat16), "tp"
-    ).astype(jnp.float32)
-    middle = flat_rows + attn_total
-    normed_rows = rms_norm(middle, mlp_gain)
-    gate_val = jnp.dot(normed_rows, gate_weight, preferred_element_type=jnp.float32)
-    up_val = jnp.dot(normed_rows, up_weight, preferred_element_type=jnp.float32)
+    attn_partial = jnp.dot(attended, out_weight, preferred_element_type=jnp.float32).astype(bf)
+    attn_mine = tp_reduce_scatter(attn_partial, core_bit, chip_bit)
+    quarter_rows = tok_rows // tp_count
+    row_start = (core_bit * 2 + chip_bit) * quarter_rows
+    middle = lax.dynamic_slice_in_dim(flat_rows, row_start, quarter_rows, 0) + attn_mine
+    normed_mine = rms_norm(middle, mlp_gain)
+    normed_rows = tp_all_gather(normed_mine, core_bit, chip_bit)
+    gate_up = jnp.dot(normed_rows, gate_up_weight, preferred_element_type=jnp.float32)
+    gate_val = gate_up[:, :ff_cols]
+    up_val = gate_up[:, ff_cols:]
     hidden_ff = (jax.nn.silu(gate_val) * up_val).astype(jnp.bfloat16)
-    ffn_total = lax.psum(
-        jnp.dot(hidden_ff, down_weight, preferred_element_type=jnp.float32).astype(jnp.bfloat16),
-        "tp",
-    ).astype(jnp.float32)
-    result = (middle + ffn_total).astype(jnp.bfloat16)
+    ffn_partial = jnp.dot(hidden_ff, down_weight, preferred_element_type=jnp.float32).astype(bf)
+    ffn_mine = tp_reduce_scatter(ffn_partial, core_bit, chip_bit)
+    result_mine = (middle + ffn_mine).astype(jnp.bfloat16)
+    result = tp_all_gather(result_mine, core_bit, chip_bit)
     return (result.reshape(prompt_batch, sequence_length, model_width), kv_cache)
 
 

time: 378 us -> 295 us (0.78)
  waiting for transfers between devices: 234 us -> 163 us
  local copies, waits for them, and re-layouts: 53.4 us -> 35 us
  starting transfers between devices: 9.81 us -> 18.1 us
  matrix products: 44.6 us -> 38 us
  other arithmetic: 21.1 us -> 25.1 us
    psum x2 -> x0, waiting for transfers between devices: 116 us -> none  [the longest x1 60.5 us: local(): lax.psum(jnp.dot(hidden_ff, down_weight, preferred_element_type=jnp.float...]
    ppermute x0 -> x8, waiting for transfers between devices: none -> 83.7 us  [the longest x2 43.4 us: tp_reduce_scatter(): got = lax.ppermute(sent, 'tp', CROSS_PAIRS)]
    all_gather x1 -> x2, waiting for transfers between devices: 117 us -> 77.8 us  [the longest x1 77.1 us: local(): attn_all = lax.all_gather(attn_pack, 'req', axis=0, tiled=True)]
    reshape x4 -> x5, local copies, waits for them, and re-layouts: 19.8 us -> 6.7 us  [the longest x1 3.21 us: local(): qkv[:, q_cols:q_cols + kv_cols]]
    all_gather x1 -> x0, local copies, waits for them, and re-layouts: 9.91 us -> none  [local(): gathered = lax.all_gather(packed, 'req', axis=0, tiled=False)]
    dot_general x4 -> x0, local copies, waits for them, and re-layouts: 9.37 us -> none  [the longest x2 5.5 us: local(): jnp.dot(normalized_input, value_weight, preferred_element_type=jnp.float32)]
    ppermute x0 -> x8, starting transfers between devices: none -> 8.33 us  [the longest x2 3.57 us: tp_reduce_scatter(): got = lax.ppermute(pick(halves, 1 - core_bit), 'tp', CHIP_PAIRS)]
    dot_general x1, matrix products: 11.6 us -> 3.56 us  [local(): jnp.dot(hidden_ff, down_weight, preferred_element_type=jnp.float32)]
  transfers between devices with their start and end apart: 5 -> 12, of which waited for: 5 -> 9; matrix products, arithmetic and copies ran while one was open for 5% -> 25% of each run, Pallas kernels for 0% -> 0%
where the time goes in v2:
time: 295 us; the launch traced here: 294 us
  waiting for transfers between devices  163 us (55%)
  matrix products  38 us (13%)
  local copies, waits for them, and re-layouts  35 us (12%)
  other arithmetic  25.1 us (9%)
  starting transfers between devices  18.1 us (6%)
  between operations  14.5 us (5%)
    all_gather x1, waiting for transfers between devices, local(): attn_all = lax.all_gather(attn_pack, 'req', axis=0, tiled=True)  77.1 us
    ppermute x2, waiting for transfers between devices, tp_reduce_scatter(): got = lax.ppermute(sent, 'tp', CROSS_PAIRS)  43.4 us
    ppermute x2, waiting for transfers between devices, tp_all_gather(): got = lax.ppermute(quarter, 'tp', CROSS_PAIRS)  34.7 us
    sub x1, matrix products, local(): expo = jnp.exp(scores - highest)  9.64 us
    dot_general x1, matrix products, local(): jnp.dot(normed_rows, gate_up_weight, preferred_element_type=jnp.float32)  8.16 us
  transfers between devices with their start and end apart: 12, of which 9 were waited for; matrix products, arithmetic and copies ran while one was open for 25% of the time, Pallas kernels for 0%

profile of v2, /device:TPU:1, one launch (start us, length us, event | category | flops | bytes accessed | tf_op | source)
XLA Modules:
  0.0 293.9 jit_solution(7065172421199209140)
XLA Ops:
  7.2 1.0 convert.74
  8.2 1.0 convert.75
  9.1 0.9 convert.71
  12.2 4.8 %all-to-all-start = ((bf16[4,10,2752]{2,1,0:T(8,128)(2,1)}), bf16[4,10,2752]{2,1,0:T(8,128)(2,1)S(1)}, u32[]{:S(2)}, u32[]{:S(2)}) async-start(bf16[4,10,2752]{2,1,0:T(8,128)(2,1)} %pad_maximum_fusion.8), calls=%async_computation | async-start | bytes 720896 | tf_op jit(solution)/shard_map/all_to_all | solution.py:113
  17.3 4.9 %collective-permute-start = (bf16[48640]{0:T(1024)(128)(2,1)S(1)}, bf16[48640]{0:T(1024)(128)(2,1)S(1)}, u32[]{:S(2)}, u32[]{:S(2)}) collective-permute-start(bf16[48640]{0:T(1024)(128)(2,1)S(1)} %pad_maximum_fusion.11), channel_id=1, source_target_pairs={{0,0},{1,4},{2,8},{3,12},{4,16},{5,20},{6,24},{7,28},{8,32},{9,36}... | collective-permute-start | bytes 291848 | tf_op jit(solution)/shard_map/ppermute | solution.py:126
  22.2 1.6 collective-permute-done
  27.0 1.1 broadcast_and_fusion
  28.1 77.1 %all-gather.3.cloned.1.call-done = bf16[1280,1280]{1,0:T(8,128)(2,1)} async-done(((bf16[40,1280]{1,0:T(8,128)(2,1)}), bf16[1280,1280]{1,0:T(8,128)(2,1)}) %all-gather.3.cloned.1.call-update) | async-done | bytes 3276816 | tf_op jit(solution)/shard_map/all_gather | solution.py:134
  105.2 4.7 %fusion.9 = f32[1024,960]{0,1:T(8,128)S(1)} fusion(bf16[1280,1280]{1,0:T(8,128)(2,1)} %all-gather.3.cloned.1.call-done, f32[1280]{0:T(1024)S(1)} %copy-done.12, f32[1024]{0:T(1024)S(1)} %bitcast.110, bf16[1024,1280]{1,0:T(8,128)(2,1)S(1)} %bitcast.95), kind=kOutput, calls=%fused_computation.17 | convolution fusion | flops 2521825280 | bytes 9184256 | tf_op jit(solution)/shard_map/dot_general | solution.py:146
  110.0 1.7 fusion.53
  111.7 3.2 %reshape.493 = f32[2,512,5,64]{1,0,3,2:T(2,128)} reshape(f32[1024,320]{0,1:T(8,128)} %get-tuple-element.5) | data formatting | bytes 2621440 | tf_op jit(solution)/shard_map/reshape | solution.py:148
  114.9 3.2 %reshape.492 = f32[2,512,5,64]{1,0,3,2:T(2,128)} reshape(f32[1024,320]{0,1:T(8,128)} %get-tuple-element.4) | data formatting | bytes 2621440 | tf_op jit(solution)/shard_map/reshape | solution.py:147
  118.1 1.3 convert_element_type.141
  119.5 1.8 fusion.55
  122.1 1.1 subtract_convert_fusion
  123.2 1.5 fusion.27
  124.8 1.8 fusion.29
  126.6 9.6 %fusion.56 = (f32[2,5,512]{2,1,0:T(8,128)S(1)}, f32[2,5,512,512]{2,3,1,0:T(8,128)}) fusion(pred[2,512,512]{1,2,0:T(8,128)(4,1)} %broadcast_and_fusion, bf16[2,512,5,32]{1,3,2,0:T(8,128)(2,1)} %get-tuple-element.7, bf16[2,512,5,32]{1,3,2,0:T(8,128)(2,1)} %get-tuple-element.6, bf16[5,2,512,64]{2,0,3,1:T(8,128)(2,1)} %fusion.27), kind=kOutput, calls=%fused_computation.110 | convolution fusion | flops 347341312 | bytes 12341248 | tf_op jit(solution)/shard_map/sub | solution.py:187
  136.2 5.6 %fusion.24 = bf16[2,512,5,64]{1,3,2,0:T(8,128)(2,1)S(1)} fusion(f32[2,5,512,512]{2,3,1,0:T(8,128)} %get-tuple-element.29, f32[2,5,512]{2,1,0:T(8,128)S(1)} %get-tuple-element.28, bf16[5,2,512,64]{2,0,3,1:T(8,128)(2,1)} %fusion.29), kind=kOutput, calls=%fused_computation.50 | convolution fusion | flops 341114880 | bytes 11816960 | tf_op jit(solution)/shard_map/phqk,pkhd->pqhd/dot_general | solution.py:190
  142.5 0.9 copy.40
  143.4 2.6 slice.158
  146.0 2.7 reshape_reshape.6
  148.8 2.9 convolution_convert_fusion.1
  151.7 1.5 copy-done.6
  153.2 1.1 dynamic-slice_bitcast_fusion.1
  154.4 1.8 collective-permute-start.1
  156.2 3.0 %collective-permute-done.1 = bf16[512,1280]{1,0:T(8,128)(2,1)} collective-permute-done((bf16[512,1280]{1,0:T(8,128)(2,1)}, bf16[512,1280]{1,0:T(8,128)(2,1)}, u32[]{:S(2)}, u32[]{:S(2)}) %collective-permute-start.1) | collective-permute-done | bytes 1310752 | tf_op jit(solution)/shard_map/ppermute | solution.py:51
  159.2 2.0 convert_add_fusion.1
  161.2 1.5 copy-done.1
  162.7 0.9 fusion.31
  164.1 2.7 convert.90
  166.9 27.5 %collective-permute-done.2 = bf16[256,1280]{1,0:T(8,128)(2,1)} collective-permute-done((bf16[256,1280]{1,0:T(8,128)(2,1)}, bf16[256,1280]{1,0:T(8,128)(2,1)}, u32[]{:S(2)}, u32[]{:S(2)}) %collective-permute-start.2) | collective-permute-done | bytes 655392 | tf_op jit(solution)/shard_map/ppermute | solution.py:55
  194.4 2.2 multiply_reduce_fusion.1
  197.5 19.9 %collective-permute-done.3 = bf16[256,1280]{1,0:T(8,128)(2,1)S(1)} collective-permute-done((bf16[256,1280]{1,0:T(8,128)(2,1)S(1)}, bf16[256,1280]{1,0:T(8,128)(2,1)S(1)}, u32[]{:S(2)}, u32[]{:S(2)}) %collective-permute-start.3) | collective-permute-done | bytes 655392 | tf_op jit(solution)/shard_map/ppermute | solution.py:60
  217.4 1.6 maximum_select_fusion.3
  219.0 0.8 collective-permute-start.4
  220.6 3.2 %slice.164 = bf16[1280,896]{1,0:T(8,128)(2,1)} slice(bf16[1280,2688]{1,0:T(8,128)(2,1)} %all-gather.5.cloned.1.call-done), slice={[0:1280], [1792:2688]} | slice | bytes 4587520 | tf_op jit(solution)/shard_map/slice | solution.py:139
  223.8 5.1 %reshape_reshape.7 = bf16[896,1280]{1,0:T(8,128)(2,1)} reshape(bf16[1280,896]{1,0:T(8,128)(2,1)} %slice.164) | data formatting | bytes 4587520 | tf_op jit(solution)/shard_map/reshape;reshape | solution.py:139
  228.9 8.2 %fusion.6 = f32[1024,1792]{1,0:T(8,128)S(1)} fusion(bf16[1280,2688]{1,0:T(8,128)(2,1)} %all-gather.5.cloned.1.call-done, bf16[512,1280]{1,0:T(8,128)(2,1)S(1)} %collective-permute-done.4, bf16[512,1280]{1,0:T(8,128)(2,1)} %maximum_select_fusion.3, pred[]{:T(512)S(6)} %eq.12), kind=kOutput, calls=%fused_computation.11 | convolution fusion | flops 4709416960 | bytes 14548993 | tf_op jit(solution)/shard_map/dot_general | solution.py:201
  237.1 3.6 %convolution_convert_fusion = bf16[1024,1280]{1,0:T(8,128)(2,1)S(1)} fusion(bf16[896,1280]{1,0:T(8,128)(2,1)S(1)} %copy-done.7, f32[1024,1792]{1,0:T(8,128)S(1)} %fusion.6), kind=kOutput, calls=%fused_computation.13 | convolution fusion | flops 2355625984 | bytes 12255232 | tf_op jit(solution)/shard_map/dot_general | solution.py:205
  240.8 1.7 collective-permute-start.5
  242.5 2.7 collective-permute-done.5
  245.7 15.9 %collective-permute-done.6 = bf16[256,1280]{1,0:T(8,128)(2,1)S(1)} collective-permute-done((bf16[256,1280]{1,0:T(8,128)(2,1)S(1)}, bf16[256,1280]{1,0:T(8,128)(2,1)S(1)}, u32[]{:S(2)}, u32[]{:S(2)}) %collective-permute-start.6) | collective-permute-done | bytes 655392 | tf_op jit(solution)/shard_map/ppermute | solution.py:55
  262.2 14.8 %collective-permute-done.7 = bf16[256,1280]{1,0:T(8,128)(2,1)S(1)} collective-permute-done((bf16[256,1280]{1,0:T(8,128)(2,1)S(1)}, bf16[256,1280]{1,0:T(8,128)(2,1)S(1)}, u32[]{:S(2)}, u32[]{:S(2)}) %collective-permute-start.7) | collective-permute-done | bytes 655392 | tf_op jit(solution)/shard_map/ppermute | solution.py:60
  277.6 2.2 collective-permute-start.8
  279.7 1.2 copy.34
  281.2 2.6 pad_maximum_fusion
  283.9 3.2 %maximum_select_fusion.2 = bf16[1024,1280]{1,0:T(8,128)(2,1)} fusion(bf16[512,1280]{1,0:T(8,128)(2,1)} %collective-permute-done.8, bf16[512,1280]{1,0:T(8,128)(2,1)S(1)} %maximum_select_fusion.4, pred[]{:T(512)S(6)} %eq.12), kind=kLoop, calls=%fused_computation.25 | loop fusion | flops 11796480 | bytes 5242881 | tf_op jit(solution)/shard_map/jit(_where)/select_n | solution.py:67
  (79 shorter events, 11.3 us)
Async XLA Ops:
  7.2 9.8 %copy-start.8 = (f32[28,1280]{1,0:T(8,128)S(1)}, f32[28,1280]{1,0:T(8,128)}, u32[]{:S(2)}) copy-start(f32[28,1280]{1,0:T(8,128)} %param.21) | copy-start | bytes 430084
  7.2 10.0 %copy-start.9 = (f32[10,1280]{1,0:T(8,128)S(1)}, f32[10,1280]{1,0:T(8,128)}, u32[]{:S(2)}) copy-start(f32[10,1280]{1,0:T(8,128)} %param.18) | copy-start | bytes 153604
  11.0 14.8 %copy-start = (bf16[2,512,1280]{2,1,0:T(8,128)(2,1)S(1)}, bf16[2,512,1280]{2,1,0:T(8,128)(2,1)}, u32[]{:S(2)}) copy-start(bf16[2,512,1280]{2,1,0:T(8,128)(2,1)} %param.11) | copy-start | bytes 7864324
  12.2 11.7 %all-to-all-start = ((bf16[4,10,2752]{2,1,0:T(8,128)(2,1)}), bf16[4,10,2752]{2,1,0:T(8,128)(2,1)S(1)}, u32[]{:S(2)}, u32[]{:S(2)}) async-start(bf16[4,10,2752]{2,1,0:T(8,128)(2,1)} %pad_maximum_fusion.8), calls=%async_computation | async-start | bytes 720896 | tf_op jit(solution)/shard_map/all_to_all | solution.py:113
  17.0 88.2 %all-gather.3.cloned.1.call-start = ((), (), s32[]{:S(2)}) async-start(), calls=%async_computation.1 | async-start | bytes 3379200 | tf_op jit(solution)/shard_map/all_gather | solution.py:134
  17.3 6.5 %collective-permute-start = (bf16[48640]{0:T(1024)(128)(2,1)S(1)}, bf16[48640]{0:T(1024)(128)(2,1)S(1)}, u32[]{:S(2)}, u32[]{:S(2)}) collective-permute-start(bf16[48640]{0:T(1024)(128)(2,1)S(1)} %pad_maximum_fusion.11), channel_id=1, source_target_pairs={{0,0},{1,4},{2,8},{3,12},{4,16},{5,20},{6,24},{7,28},{8,32},{9,36}... | collective-permute-start | bytes 291848 | tf_op jit(solution)/shard_map/ppermute | solution.py:126
  23.9 2.7 copy-start.11
  24.8 80.4 %copy-start.12 = (f32[1280]{0:T(1024)S(1)}, f32[1280]{0:T(1024)}, u32[]{:S(2)}) copy-start(f32[1280]{0:T(1024)} %param.13) | copy-start | bytes 15364
  24.8 195.7 %all-gather.5.cloned.1.call-start = ((), (), s32[]{:S(2)}) async-start(), calls=%async_computation.2 | async-start | bytes 7096320 | tf_op jit(solution)/shard_map/all_gather | solution.py:135
  110.0 8.1 %copy-start.2 = (bf16[1024,320]{0,1:T(8,128)(2,1)}, bf16[1024,320]{0,1:T(8,128)(2,1)S(1)}, u32[]{:S(2)}) copy-start(bf16[1024,320]{0,1:T(8,128)(2,1)S(1)} %slice.188) | copy-start | bytes 1966084
  119.4 2.2 copy-start.4
  122.1 2.7 copy-start.5
  151.7 1.5 copy-start.6
  154.4 4.8 %collective-permute-start.1 = (bf16[512,1280]{1,0:T(8,128)(2,1)}, bf16[512,1280]{1,0:T(8,128)(2,1)}, u32[]{:S(2)}, u32[]{:S(2)}) collective-permute-start(bf16[512,1280]{1,0:T(8,128)(2,1)} %dynamic-slice_bitcast_fusion.1), channel_id=1, source_target_pairs={{0,1},{1,0},{2,3},{3,2},{4,5},{5,4},{6,7},{7,6},{8,9},{9,8},{10,11... | collective-permute-start | bytes 3932168 | tf_op jit(solution)/shard_map/ppermute | solution.py:51
  161.2 1.5 copy-start.1
  163.6 30.8 %collective-permute-start.2 = (bf16[256,1280]{1,0:T(8,128)(2,1)}, bf16[256,1280]{1,0:T(8,128)(2,1)}, u32[]{:S(2)}, u32[]{:S(2)}) collective-permute-start(bf16[256,1280]{1,0:T(8,128)(2,1)} %fusion.31), channel_id=1, source_target_pairs={{0,2},{2,0},{1,3},{3,1},{4,6},{6,4},{5,7},{7,5},{8,10},{10,8},{9,1... | collective-permute-start | bytes 1966088 | tf_op jit(solution)/shard_map/ppermute | solution.py:55
  166.9 29.7 %copy-start.10 = (f32[1280]{0:T(1024)S(1)}, f32[1280]{0:T(1024)}, u32[]{:S(2)}) copy-start(f32[1280]{0:T(1024)} %param.14) | copy-start | bytes 15364
  196.8 20.6 %collective-permute-start.3 = (bf16[256,1280]{1,0:T(8,128)(2,1)S(1)}, bf16[256,1280]{1,0:T(8,128)(2,1)S(1)}, u32[]{:S(2)}, u32[]{:S(2)}) collective-permute-start(bf16[256,1280]{1,0:T(8,128)(2,1)S(1)} %multiply_convert_fusion.2), channel_id=1, source_target_pairs={{0,2},{2,0},{1,3},{3,1},{4,6},{6,4},{5,7},{7,5},{8,10},{10,8},{9,1... | collective-permute-start | bytes 1966088 | tf_op jit(solution)/shard_map/ppermute | solution.py:60
  219.0 9.9 %collective-permute-start.4 = (bf16[512,1280]{1,0:T(8,128)(2,1)}, bf16[512,1280]{1,0:T(8,128)(2,1)S(1)}, u32[]{:S(2)}, u32[]{:S(2)}) collective-permute-start(bf16[512,1280]{1,0:T(8,128)(2,1)} %maximum_select_fusion.3), channel_id=1, source_target_pairs={{0,1},{1,0},{2,3},{3,2},{4,5},{5,4},{6,7},{7,6},{8,9},{9,8},{10,11... | collective-permute-start | bytes 3932168 | tf_op jit(solution)/shard_map/ppermute | solution.py:66
  228.9 8.2 %copy-start.7 = (bf16[896,1280]{1,0:T(8,128)(2,1)S(1)}, bf16[896,1280]{1,0:T(8,128)(2,1)}, u32[]{:S(2)}) copy-start(bf16[896,1280]{1,0:T(8,128)(2,1)} %reshape_reshape.7) | copy-start | bytes 6881284
  240.8 4.4 %collective-permute-start.5 = (bf16[512,1280]{1,0:T(8,128)(2,1)S(1)}, bf16[512,1280]{1,0:T(8,128)(2,1)S(1)}, u32[]{:S(2)}, u32[]{:S(2)}) collective-permute-start(bf16[512,1280]{1,0:T(8,128)(2,1)S(1)} %dynamic-slice_bitcast_fusion), channel_id=1, source_target_pairs={{0,1},{1,0},{2,3},{3,2},{4,5},{5,4},{6,7},{7,6},{8,9},{9,8},{10,11... | collective-permute-start | bytes 3932168 | tf_op jit(solution)/shard_map/ppermute | solution.py:51
  245.6 34.1 %copy-start.3 = (bf16[1024,320]{0,1:T(8,128)(2,1)S(1)}, bf16[1024,320]{0,1:T(8,128)(2,1)}, u32[]{:S(2)}) copy-start(bf16[1024,320]{0,1:T(8,128)(2,1)} %copy-done.2) | copy-start | bytes 1966084
  245.6 16.0 %collective-permute-start.6 = (bf16[256,1280]{1,0:T(8,128)(2,1)S(1)}, bf16[256,1280]{1,0:T(8,128)(2,1)S(1)}, u32[]{:S(2)}, u32[]{:S(2)}) collective-permute-start(bf16[256,1280]{1,0:T(8,128)(2,1)S(1)} %fusion.32), channel_id=1, source_target_pairs={{0,2},{2,0},{1,3},{3,1},{4,6},{6,4},{5,7},{7,5},{8,10},{10,8},{9,1... | collective-permute-start | bytes 1966088 | tf_op jit(solution)/shard_map/ppermute | solution.py:55
  261.9 15.1 %collective-permute-start.7 = (bf16[256,1280]{1,0:T(8,128)(2,1)S(1)}, bf16[256,1280]{1,0:T(8,128)(2,1)S(1)}, u32[]{:S(2)}, u32[]{:S(2)}) collective-permute-start(bf16[256,1280]{1,0:T(8,128)(2,1)S(1)} %fusion.22), channel_id=1, source_target_pairs={{0,2},{2,0},{1,3},{3,1},{4,6},{6,4},{5,7},{7,5},{8,10},{10,8},{9,1... | collective-permute-start | bytes 1966088 | tf_op jit(solution)/shard_map/ppermute | solution.py:60
  277.6 6.3 %collective-permute-start.8 = (bf16[512,1280]{1,0:T(8,128)(2,1)S(1)}, bf16[512,1280]{1,0:T(8,128)(2,1)}, u32[]{:S(2)}, u32[]{:S(2)}) collective-permute-start(bf16[512,1280]{1,0:T(8,128)(2,1)S(1)} %maximum_select_fusion.4), channel_id=1, source_target_pairs={{0,1},{1,0},{2,3},{3,2},{4,5},{5,4},{6,7},{7,6},{8,9},{9,8},{10,11... | collective-permute-start | bytes 3932168 | tf_op jit(solution)/shard_map/ppermute | solution.py:66
Sparse Core Ops, SparseCore 0:
  24.9 80.1 all-gather.2
  108.2 112.3 all-gather.4
